TPU v7x, 256 devices: a whole 4x4x8 slice. The times are simulated.
256 devices in a mesh: seq: 32 (over z, x), dp: 8 (over y, core).
Axes of the slice: x: 4, y: 4, z: 8, core: 2. Of those that a mesh axis runs over, the one named last changes fastest.
Arguments:
- query_rows: bfloat16 [8, 4096, 2048], P('dp', 'seq'), may hold values from -6 to 6
- key_rows: bfloat16 [8, 4096, 2048], P('dp', 'seq'), may hold values from -6 to 6
- value_rows: bfloat16 [8, 4096, 2048], P('dp', 'seq'), may hold values from -6 to 6
- out_grad: bfloat16 [8, 4096, 4096], P('dp', 'seq'), may hold values from -6 to 6
- rand_blocks: int32 [8, 64, 3], P('dp'), may hold values from 0 to 63
- global_tokens: int32 [8, 128], P('dp'), may hold values from 0 to 4095, as said below
- out_proj: bfloat16 [2048, 4096], P('dp'), may hold values from -0.125 to 0.125
Outputs:
- grad_queries: bfloat16 [8, 4096, 2048], P('dp', 'seq')
- grad_keys: bfloat16 [8, 4096, 2048], P('dp', 'seq')
- grad_values: bfloat16 [8, 4096, 2048], P('dp', 'seq')
- grad_out_proj: bfloat16 [2048, 4096], P('dp')
Inputs may be any that keep to these rules, and one draw needn't show every extreme that they name: `global_tokens`: in each document window 128 distinct positions in increasing order; the first and the last position of the window are always among them.
All inputs are finite; a program needn't handle non-finite values.
Results may differ from a plain program's by a relative error of at most 0.012.
Values may be sent and summed in bfloat16 or wider, within the bound.
No kernel may reach another device: no remote copies, remote signals or barrier semaphores. Data moves between devices by JAX's collectives and lax.ppermute only.
A program may use at most 128 MiB of HBM per device.

v0:
```python
import math

import jax
import jax.numpy as jnp
from jax import lax
from jax.sharding import Mesh, PartitionSpec as P

HEAD_DIM = 128
BLOCK = 64
RANDOM = 3


MASKED = -1e30
SEQ_AXES = ("sz", "sx")
DP_AXES = ("dy", "dc")


def softmax_rows(scores):
    highest = jnp.max(scores, axis=-1, keepdims=True)
    raised = jnp.exp(scores - highest)
    return raised / jnp.sum(raised, axis=-1, keepdims=True)


def shards(query_rows, key_rows, value_rows, out_grad, rand_blocks, global_tokens, out_proj):
    seq_devices = lax.axis_size(SEQ_AXES)
    dp_devices = lax.axis_size(DP_AXES)
    tokens = query_rows.shape[1]
    width = query_rows.shape[2]
    model_width = out_grad.shape[2]
    head_count = width // HEAD_DIM
    splitting = max(seq_devices // head_count, 1)
    heads_here = max(head_count // seq_devices, 1)
    columns = heads_here * HEAD_DIM
    head_groups = seq_devices // splitting
    slice_rows = tokens // splitting
    seq_length = tokens * seq_devices
    block_total = seq_length // BLOCK
    window_keys = (3 + RANDOM) * BLOCK
    query_count = seq_devices * slice_rows
    query_blocks = query_count // BLOCK
    owned_groups = seq_devices // dp_devices // splitting
    global_count = global_tokens.shape[1]
    scaling = 1.0 / math.sqrt(HEAD_DIM)
    my_slice = lax.axis_index(SEQ_AXES) % splitting
    doc_blocks = rand_blocks[0]
    doc_globals = global_tokens[0]
    def head_rows(rows):
        return (
            rows[0]
            .reshape(splitting, slice_rows, head_groups, columns)
            .transpose(2, 0, 1, 3)
            .reshape(seq_devices, slice_rows, columns)
        )

    partner = [(i, i ^ 1) for i in range(lax.axis_size("sx"))]

    def both_halves(mine):
        other = lax.ppermute(mine, "sx", partner)
        low = jnp.where(my_slice == 0, mine, other)
        high = jnp.where(my_slice == 0, other, mine)
        return jnp.stack([low, high], axis=1).reshape(seq_devices, tokens, columns)

    def to_heads(rows):
        return lax.all_to_all(head_rows(rows), SEQ_AXES, split_axis=0, concat_axis=0, tiled=True)

    query_head = to_heads(query_rows)
    key_head = both_halves(to_heads(key_rows))
    value_head = both_halves(to_heads(value_rows))
    source_start = jnp.arange(seq_devices, dtype=jnp.int32)[:, None] * tokens
    offsets = jnp.arange(slice_rows, dtype=jnp.int32)[None, :]
    query_pos = (source_start + my_slice * slice_rows + offsets).reshape(query_count)
    block_of = query_pos.reshape(query_blocks, BLOCK)[:, 0] // BLOCK
    window = block_of[:, None] + jnp.arange(-1, 2, dtype=jnp.int32)[None, :]
    inside = (window >= 0) & (window < block_total)
    block_ids = jnp.concatenate(
        [jnp.clip(window, 0, block_total - 1), jnp.take(doc_blocks, block_of, axis=0)], axis=1
    )
    usable = jnp.concatenate(
        [jnp.repeat(inside, BLOCK, axis=1), jnp.ones((query_blocks, RANDOM * BLOCK), dtype=bool)],
        axis=1,
    )
    key_all = key_head.reshape(seq_length, heads_here, HEAD_DIM)
    value_all = value_head.reshape(seq_length, heads_here, HEAD_DIM)
    key_win = key_all.reshape(block_total, BLOCK, heads_here, HEAD_DIM)[block_ids].reshape(
        query_blocks, window_keys, heads_here, HEAD_DIM
    )
    value_win = value_all.reshape(block_total, BLOCK, heads_here, HEAD_DIM)[block_ids].reshape(
        query_blocks, window_keys, heads_here, HEAD_DIM
    )
    key_glob = jnp.take(key_all, doc_globals, axis=0)
    value_glob = jnp.take(value_all, doc_globals, axis=0)
    query_blk = query_head.reshape(query_blocks, BLOCK, heads_here, HEAD_DIM)
    score_win = (
        jnp.einsum("bqhe,bkhe->bhqk", query_blk, key_win, preferred_element_type=jnp.float32)
        * scaling
    )
    score_win = jnp.where(usable[:, None, None, :], score_win, MASKED)
    score_glob = (
        jnp.einsum("bqhe,khe->bhqk", query_blk, key_glob, preferred_element_type=jnp.float32)
        * scaling
    )
    prob_rows = softmax_rows(jnp.concatenate([score_win, score_glob], axis=-1))
    prob_bf = prob_rows.astype(jnp.bfloat16)
    sparse_out = jnp.einsum(
        "bhqk,bkhe->bqhe", prob_bf[..., :window_keys], value_win, preferred_element_type=jnp.float32
    )
    sparse_out = sparse_out + jnp.einsum(
        "bhqk,khe->bqhe", prob_bf[..., window_keys:], value_glob, preferred_element_type=jnp.float32
    )
    matches = query_pos[:, None] == doc_globals[None, :]
    picker = matches.astype(jnp.bfloat16)
    picker_f = matches.astype(jnp.float32)
    is_global = jnp.any(matches, axis=1)
    query_glob = (
        jnp.einsum(
            "ng,nc->gc",
            picker,
            query_head.reshape(query_count, columns),
            preferred_element_type=jnp.float32,
        )
        .astype(jnp.bfloat16)
        .reshape(global_count, heads_here, HEAD_DIM)
    )
    prob_glob = softmax_rows(
        jnp.einsum("ghe,the->hgt", query_glob, key_all, preferred_element_type=jnp.float32)
        * scaling
    )
    prob_glob_bf = prob_glob.astype(jnp.bfloat16)
    glob_out = jnp.einsum(
        "hgt,the->ghe", prob_glob_bf, value_all, preferred_element_type=jnp.float32
    ).reshape(global_count, columns)
    placed = jnp.dot(picker_f, glob_out, precision=lax.Precision.HIGHEST)
    attention = jnp.where(
        is_global[:, None], placed, sparse_out.reshape(query_count, columns)
    ).astype(jnp.bfloat16)
    owned = lax.all_to_all(
        lax.all_to_all(
            attention.reshape(1, seq_devices, slice_rows, columns),
            SEQ_AXES,
            split_axis=1,
            concat_axis=1,
            tiled=True,
        ),
        DP_AXES,
        split_axis=1,
        concat_axis=0,
        tiled=True,
    )
    owned = owned.reshape(dp_devices, owned_groups, splitting, slice_rows, columns)
    proj_rows = out_proj.reshape(owned_groups, columns, model_width)
    piece_rows = lax.all_gather(out_grad, DP_AXES, axis=0, tiled=True)
    doc_count = piece_rows.shape[0]
    grads = piece_rows.reshape(doc_count, splitting, slice_rows, model_width)
    local_delta = jnp.einsum(
        "kptd,gcd->kgptc", grads, proj_rows, preferred_element_type=jnp.float32
    ).astype(jnp.bfloat16)
    local_delta = local_delta.reshape(doc_count, owned_groups * splitting, slice_rows, columns)
    delta_blocks = local_delta
    grad_sum = jnp.einsum("kgptc,kptd->gcd", owned, grads, preferred_element_type=jnp.float32)
    grad_sum, delta_blocks = (grad_sum, delta_blocks)
    z_size = lax.axis_size("sz")
    x_size = lax.axis_size("sx")
    proj_part = grad_sum.reshape(width // dp_devices, model_width).astype(jnp.bfloat16)
    z_rows = proj_part.shape[0] // (x_size * z_size)
    x_sum = jnp.sum(
        lax.all_to_all(
            proj_part.reshape(z_size, x_size, z_rows, model_width).transpose(1, 0, 2, 3),
            "sx",
            0,
            0,
            tiled=True,
        ).astype(jnp.float32),
        axis=0,
    )
    z_sum = jnp.sum(
        lax.all_to_all(
            x_sum.astype(jnp.bfloat16).reshape(z_size, z_rows, model_width), "sz", 0, 0, tiled=True
        ).astype(jnp.float32),
        axis=0,
    )
    grad_out_proj = lax.all_gather(z_sum.astype(jnp.bfloat16), SEQ_AXES, axis=0, tiled=True)
    delta_head = lax.all_to_all(
        lax.all_to_all(delta_blocks, DP_AXES, split_axis=0, concat_axis=1, tiled=True),
        SEQ_AXES,
        split_axis=1,
        concat_axis=1,
        tiled=True,
    )
    delta_blk = delta_head.reshape(query_blocks, BLOCK, heads_here, HEAD_DIM)
    prob_grad = jnp.concatenate(
        [
            jnp.einsum("bqhe,bkhe->bhqk", delta_blk, value_win, preferred_element_type=jnp.float32),
            jnp.einsum("bqhe,khe->bhqk", delta_blk, value_glob, preferred_element_type=jnp.float32),
        ],
        axis=-1,
    )
    keep_rows = (
        jnp.where(is_global, 0.0, 1.0).astype(jnp.float32).reshape(query_blocks, 1, BLOCK, 1)
    )
    score_bf = (
        prob_rows * (prob_grad - jnp.sum(prob_rows * prob_grad, axis=-1, keepdims=True)) * keep_rows
    ).astype(jnp.bfloat16)
    prob_kept = prob_bf * keep_rows.astype(jnp.bfloat16)
    grad_query = jnp.einsum(
        "bhqk,bkhe->bqhe", score_bf[..., :window_keys], key_win, preferred_element_type=jnp.float32
    )
    grad_query = (
        grad_query
        + jnp.einsum(
            "bhqk,khe->bqhe",
            score_bf[..., window_keys:],
            key_glob,
            preferred_element_type=jnp.float32,
        )
    ) * scaling
    flat_ids = block_ids.reshape(-1)
    key_part = (
        jnp.einsum(
            "bhqk,bqhe->bkhe",
            score_bf[..., :window_keys],
            query_blk,
            preferred_element_type=jnp.float32,
        )
        * scaling
    )
    key_globpart = (
        jnp.einsum(
            "bhqk,bqhe->khe",
            score_bf[..., window_keys:],
            query_blk,
            preferred_element_type=jnp.float32,
        )
        * scaling
    )
    value_part = jnp.einsum(
        "bhqk,bqhe->bkhe",
        prob_kept[..., :window_keys],
        delta_blk,
        preferred_element_type=jnp.float32,
    )
    value_globpart = jnp.einsum(
        "bhqk,bqhe->khe",
        prob_kept[..., window_keys:],
        delta_blk,
        preferred_element_type=jnp.float32,
    )
    block_hot = (block_ids[:, :, None] == jnp.arange(block_total, dtype=jnp.int32)).astype(
        jnp.float32
    )

    def place_blocks(parts):
        return jnp.einsum(
            "bjc,bjke->cke",
            block_hot,
            parts.reshape(query_blocks, 3 + RANDOM, BLOCK, columns),
            precision=lax.Precision.HIGHEST,
            preferred_element_type=jnp.float32,
        ).reshape(seq_length, columns)

    grad_key = place_blocks(key_part)
    grad_key = grad_key.at[doc_globals].add(key_globpart.reshape(global_count, columns))
    grad_value = place_blocks(value_part)
    grad_value = grad_value.at[doc_globals].add(value_globpart.reshape(global_count, columns))
    delta_glob = (
        jnp.einsum(
            "ng,nc->gc",
            picker,
            delta_head.reshape(query_count, columns),
            preferred_element_type=jnp.float32,
        )
        .astype(jnp.bfloat16)
        .reshape(global_count, heads_here, HEAD_DIM)
    )
    prob_grad_glob = jnp.einsum(
        "ghe,the->hgt", delta_glob, value_all, preferred_element_type=jnp.float32
    )
    score_glob_bf = (
        prob_glob * (prob_grad_glob - jnp.sum(prob_glob * prob_grad_glob, axis=-1, keepdims=True))
    ).astype(jnp.bfloat16)
    grad_query_glob = (
        jnp.einsum(
            "hgt,the->ghe", score_glob_bf, key_all, preferred_element_type=jnp.float32
        ).reshape(global_count, columns)
        * scaling
    )
    grad_key = (
        grad_key
        + jnp.einsum(
            "hgt,ghe->the", score_glob_bf, query_glob, preferred_element_type=jnp.float32
        ).reshape(seq_length, columns)
        * scaling
    )
    grad_value = grad_value + jnp.einsum(
        "hgt,ghe->the", prob_glob_bf, delta_glob, preferred_element_type=jnp.float32
    ).reshape(seq_length, columns)
    grad_query_all = grad_query.reshape(query_count, columns) + jnp.dot(
        picker_f, grad_query_glob, precision=lax.Precision.HIGHEST
    )
    def my_half(grads):
        halves = grads.reshape(seq_devices, splitting, slice_rows, columns)
        mine = jnp.where(my_slice == 0, halves[:, 0], halves[:, 1])
        theirs = jnp.where(my_slice == 0, halves[:, 1], halves[:, 0])
        received = lax.ppermute(theirs.astype(jnp.bfloat16), "sx", partner)
        return (mine + received.astype(jnp.float32)).astype(jnp.bfloat16)

    def to_positions(rows):
        back = lax.all_to_all(rows, SEQ_AXES, split_axis=0, concat_axis=0, tiled=True)
        return (
            back.reshape(head_groups, splitting, slice_rows, columns)
            .transpose(1, 2, 0, 3)
            .reshape(1, tokens, width)
        )

    grad_queries = to_positions(
        grad_query_all.astype(jnp.bfloat16).reshape(seq_devices, slice_rows, columns)
    )
    grad_keys = to_positions(my_half(grad_key))
    grad_values = to_positions(my_half(grad_value))
    return (grad_queries, grad_keys, grad_values, grad_out_proj)


def solution(mesh):
    seq_size, dp_size = mesh.shape["seq"], mesh.shape["dp"]
    torus = Mesh(
        mesh.devices.reshape(seq_size // 4, 4, dp_size // 2, 2), SEQ_AXES + DP_AXES
    )
    return jax.shard_map(
        shards,
        mesh=torus,
        in_specs=(
            P(DP_AXES, SEQ_AXES, None),
            P(DP_AXES, SEQ_AXES, None),
            P(DP_AXES, SEQ_AXES, None),
            P(DP_AXES, SEQ_AXES, None),
            P(DP_AXES, None, None),
            P(DP_AXES, None),
            P(DP_AXES, None),
        ),
        out_specs=(P(DP_AXES, SEQ_AXES, None), P(DP_AXES, SEQ_AXES, None), P(DP_AXES, SEQ_AXES, None), P(DP_AXES, None)),
        check_vma=False,
    )
```

profile of v0, /device:TPU:8, one launch (start us, length us, event | category | flops | bytes accessed | tf_op | source)
XLA Modules:
  0.0 389.0 jit_solution(12711608443150883492)
XLA Ops:
  10.1 11.6 %all-to-all-start = ((bf16[32,64,128]{2,1,0:T(8,128)(2,1)}), bf16[32,64,128]{2,1,0:T(8,128)(2,1)}, u32[]{:S(2)}, u32[]{:S(2)}) async-start(bf16[32,64,128]{2,1,0:T(8,128)(2,1)} %bitcast.1), calls=%async_computation | async-start | bytes 1048576 | tf_op jit(solution)/shard_map/all_to_all | solution.py:64
  22.8 16.6 %all-to-all-done = bf16[32,64,128]{2,1,0:T(8,128)(2,1)} async-done(((bf16[32,64,128]{2,1,0:T(8,128)(2,1)}), bf16[32,64,128]{2,1,0:T(8,128)(2,1)}, u32[]{:S(2)}, u32[]{:S(2)}) %all-to-all-start) | async-done | bytes 524320 | tf_op jit(solution)/shard_map/all_to_all | solution.py:64
  39.4 4.6 %all-to-all-start.4 = ((bf16[32,64,128]{2,1,0:T(8,128)(2,1)}), bf16[32,64,128]{2,1,0:T(8,128)(2,1)S(1)}, u32[]{:S(2)}, u32[]{:S(2)}) async-start(bf16[32,64,128]{2,1,0:T(8,128)(2,1)} %bitcast.34), calls=%async_computation.4 | async-start | bytes 1048576 | tf_op jit(solution)/shard_map/all_to_all | solution.py:64
  47.8 13.2 %all-to-all-done.4 = bf16[32,64,128]{2,1,0:T(8,128)(2,1)S(1)} async-done(((bf16[32,64,128]{2,1,0:T(8,128)(2,1)}), bf16[32,64,128]{2,1,0:T(8,128)(2,1)S(1)}, u32[]{:S(2)}, u32[]{:S(2)}) %all-to-all-start.4) | async-done | bytes 524320 | tf_op jit(solution)/shard_map/all_to_all | solution.py:64
  68.9 13.6 %all-to-all-done.1 = bf16[32,64,128]{2,1,0:T(8,128)(2,1)S(1)} async-done(((bf16[32,64,128]{2,1,0:T(8,128)(2,1)}), bf16[32,64,128]{2,1,0:T(8,128)(2,1)S(1)}, u32[]{:S(2)}, u32[]{:S(2)}) %all-to-all-start.1) | async-done | bytes 524320 | tf_op jit(solution)/shard_map/all_to_all | solution.py:64
  87.7 7.9 %collective-permute-done = bf16[32,64,128]{2,1,0:T(8,128)(2,1)} collective-permute-done((bf16[32,64,128]{2,1,0:T(8,128)(2,1)}, bf16[32,64,128]{2,1,0:T(8,128)(2,1)}, u32[]{:S(2)}, u32[]{:S(2)}) %collective-permute-start) | collective-permute-done | bytes 524320 | tf_op jit(solution)/shard_map/ppermute | solution.py:58
  120.5 25.7 %all_to_all.71 = bf16[1,32,64,128]{3,2,0,1:T(8,128)(2,1)} all-to-all(bf16[1,32,64,128]{3,2,0,1:T(8,128)(2,1)S(1)} %bitcast.374), channel_id=1, replica_groups=mesh['sz'=8,'sx'=4,'dy'=4,'dc'=2] {'sz','sx'}, dimensions={1} | all-to-all | bytes 1048576 | tf_op jit(solution)/shard_map/all_to_all | solution.py:137
  146.2 4.9 %all-to-all-start.9 = ((bf16[1,32,64,128]{3,2,0,1:T(8,128)(2,1)}), bf16[1,32,64,128]{3,2,0,1:T(8,128)(2,1)}, u32[]{:S(2)}, u32[]{:S(2)}) async-start(bf16[1,32,64,128]{3,2,0,1:T(8,128)(2,1)} %all_to_all.71), calls=%async_computation.9 | async-start | bytes 1048576 | tf_op jit(solution)/shard_map/all_to_all | solution.py:136
  151.1 4.9 %fusion.36 = bf16[8,2,2,64,128]{4,3,2,0,1:T(8,128)(2,1)S(1)} fusion(bf16[2,128,4096,1,1]{2,1,4,3,0:T(8,128)(2,1)S(1)} %bitcast.334, bf16[8,2,64,4096,1]{3,2,1,0,4:T(8,128)(2,1)} %bitcast.354), kind=kOutput, calls=%fused_computation.67 | convolution fusion | flops 2147745792 | bytes 11010048 | tf_op jit(solution)/shard_map/kptd,gcd->kgptc/dot_general | solution.py:154
  160.1 5.5 %all-to-all-start.2 = ((bf16[8,4,64,128]{3,2,1,0:T(8,128)(2,1)}), bf16[8,4,64,128]{3,2,1,0:T(8,128)(2,1)}, u32[]{:S(2)}, u32[]{:S(2)}) async-start(bf16[8,4,64,128]{3,2,1,0:T(8,128)(2,1)} %bitcast.29), calls=%async_computation.2 | async-start | bytes 1048576 | tf_op jit(solution)/shard_map/all_to_all | solution.py:183
  168.3 6.3 %all-to-all-done.2 = bf16[8,4,64,128]{3,2,1,0:T(8,128)(2,1)} async-done(((bf16[8,4,64,128]{3,2,1,0:T(8,128)(2,1)}), bf16[8,4,64,128]{3,2,1,0:T(8,128)(2,1)}, u32[]{:S(2)}, u32[]{:S(2)}) %all-to-all-start.2) | async-done | bytes 524320 | tf_op jit(solution)/shard_map/all_to_all | solution.py:183
  174.6 18.6 %all-to-all-start.3 = ((bf16[1,32,64,128]{3,2,0,1:T(8,128)(2,1)}), bf16[1,32,64,128]{3,2,0,1:T(8,128)(2,1)}, u32[]{:S(2)}, u32[]{:S(2)}) async-start(bf16[1,32,64,128]{3,2,0,1:T(8,128)(2,1)} %bitcast.31), calls=%async_computation.3 | async-start | bytes 1048576 | tf_op jit(solution)/shard_map/all_to_all | solution.py:182
  193.2 5.9 %fusion.4 = bf16[256,4096]{1,0:T(8,128)(2,1)S(1)} fusion(bf16[256,8,2,64]{0,3,2,1:T(8,128)(2,1)} %dot_general.135, bf16[8,2,64,4096]{3,2,1,0:T(8,128)(2,1)} %bitcast.355), kind=kOutput, calls=%fused_computation.12 | convolution fusion | flops 2148532224 | bytes 11010048 | tf_op jit(solution)/shard_map/kgptc,kptd->gcd/dot_general | solution.py:159
  200.7 9.8 %all-to-all-done.3 = bf16[1,32,64,128]{3,2,0,1:T(8,128)(2,1)} async-done(((bf16[1,32,64,128]{3,2,0,1:T(8,128)(2,1)}), bf16[1,32,64,128]{3,2,0,1:T(8,128)(2,1)}, u32[]{:S(2)}, u32[]{:S(2)}) %all-to-all-start.3) | async-done | bytes 524320 | tf_op jit(solution)/shard_map/all_to_all | solution.py:182
  224.5 7.6 %fusion.22 = f32[64,64,128]{2,0,1:T(8,128)} fusion(f32[32,6,64,128]{3,2,1,0:T(8,128)S(1)} %bitcast.344, s32[32,6]{0,1:T(8,128)S(1)} %pad_add_fusion), kind=kOutput, calls=%fused_computation.49 | convolution fusion | flops 1207971840 | bytes 8389376 | tf_op jit(solution)/shard_map/bjc,bjke->cke/dot_general | solution.py:252
  242.3 4.9 %all-to-all-start.11 = ((bf16[8,8,4096]{2,1,0:T(8,128)(2,1)}), bf16[8,8,4096]{2,1,0:T(8,128)(2,1)}, u32[]{:S(2)}, u32[]{:S(2)}) async-start(bf16[8,8,4096]{2,1,0:T(8,128)(2,1)} %reduce_sum.64), calls=%async_computation.11 | async-start | bytes 1048576 | tf_op jit(solution)/shard_map/all_to_all | solution.py:176
  263.4 4.6 %all-to-all-start.5 = ((bf16[32,64,128]{2,1,0:T(8,128)(2,1)}), bf16[32,64,128]{2,1,0:T(8,128)(2,1)}, u32[]{:S(2)}, u32[]{:S(2)}) async-start(bf16[32,64,128]{2,1,0:T(8,128)(2,1)} %bitcast.360), calls=%async_computation.5 | async-start | bytes 1048576 | tf_op jit(solution)/shard_map/all_to_all | solution.py:307
  284.3 4.7 %convolution_bitcast_fusion.2 = f32[32,384,1,128]{1,3,0,2:T(8,128)} fusion(bf16[32,1,64,512]{3,2,0,1:T(8,128)(2,1)S(1)} %copy-done.23, bf16[1,32,64,128]{3,2,0,1:T(8,128)(2,1)} %all-to-all-done.3), kind=kOutput, calls=%fused_computation.30 | convolution fusion | flops 201326592 | bytes 8388608 | tf_op jit(solution)/shard_map/bhqk,bqhe->bkhe/dot_general | solution.py:235
  289.1 6.6 %copy.152 = f32[32,384,1,128]{3,1,0,2:T(8,128)} copy(f32[32,384,1,128]{1,3,0,2:T(8,128)} %convolution_bitcast_fusion.2) | data formatting | bytes 12582912 | tf_op jit(solution)/shard_map/bhqk,bqhe->bkhe/transpose | solution.py:235
  295.6 8.7 %fusion.25 = f32[64,64,128]{2,0,1:T(8,128)S(1)} fusion(f32[32,6,64,128]{3,2,1,0:T(8,128)} %bitcast.343, s32[32,6]{0,1:T(8,128)S(1)} %pad_add_fusion), kind=kOutput, calls=%fused_computation.50 | convolution fusion | flops 1207971840 | bytes 8389376 | tf_op jit(solution)/shard_map/bjc,bjke->cke/dot_general | solution.py:252
  323.3 9.4 %all-to-all-start.6 = ((bf16[32,64,128]{2,1,0:T(8,128)(2,1)}), bf16[32,64,128]{2,1,0:T(8,128)(2,1)S(1)}, u32[]{:S(2)}, u32[]{:S(2)}) async-start(bf16[32,64,128]{2,1,0:T(8,128)(2,1)} %fusion.48), calls=%async_computation.6 | async-start | bytes 1048576 | tf_op jit(solution)/shard_map/all_to_all | solution.py:307
  336.3 16.1 %collective-permute-done.3 = bf16[32,64,128]{2,1,0:T(8,128)(2,1)S(1)} collective-permute-done((bf16[32,64,128]{2,1,0:T(8,128)(2,1)S(1)}, bf16[32,64,128]{2,1,0:T(8,128)(2,1)S(1)}, u32[]{:S(2)}, u32[]{:S(2)}) %collective-permute-start.3) | collective-permute-done | bytes 524320 | tf_op jit(solution)/shard_map/ppermute | solution.py:303
  353.4 7.4 %all-to-all-start.7 = ((bf16[32,64,128]{2,1,0:T(8,128)(2,1)}), bf16[32,64,128]{2,1,0:T(8,128)(2,1)S(1)}, u32[]{:S(2)}, u32[]{:S(2)}) async-start(bf16[32,64,128]{2,1,0:T(8,128)(2,1)} %fusion.47), calls=%async_computation.7 | async-start | bytes 1048576 | tf_op jit(solution)/shard_map/all_to_all | solution.py:307
  364.6 12.7 %all-to-all-done.7 = bf16[32,64,128]{2,1,0:T(8,128)(2,1)S(1)} async-done(((bf16[32,64,128]{2,1,0:T(8,128)(2,1)}), bf16[32,64,128]{2,1,0:T(8,128)(2,1)S(1)}, u32[]{:S(2)}, u32[]{:S(2)}) %all-to-all-start.7) | async-done | bytes 524320 | tf_op jit(solution)/shard_map/all_to_all | solution.py:307
  (173 shorter events, 142.3 us)
Async XLA Ops:
  7.2 144.0 %copy-start = (bf16[256,4096]{1,0:T(8,128)(2,1)S(1)}, bf16[256,4096]{1,0:T(8,128)(2,1)}, u32[]{:S(2)}) copy-start(bf16[256,4096]{1,0:T(8,128)(2,1)} %param.15) | copy-start | bytes 6291460
  7.2 14.5 %copy-start.24 = (bf16[1,128,2048]{2,1,0:T(8,128)(2,1)S(1)}, bf16[1,128,2048]{2,1,0:T(8,128)(2,1)}, u32[]{:S(2)}) copy-start(bf16[1,128,2048]{2,1,0:T(8,128)(2,1)} %param.11) | copy-start | bytes 1572868
  7.2 143.9 %all-gather.3.cloned.1.call-start = ((), (), s32[]{:S(2)}) async-start(), calls=%async_computation.12 | async-start | bytes 9437184 | tf_op jit(solution)/shard_map/all_gather | solution.py:151
  10.0 34.2 %copy-start.26 = (s32[1,64,3]{1,0,2:T(1,128)S(1)}, s32[1,64,3]{1,0,2:T(1,128)}, u32[]{:S(2)}) copy-start(s32[1,64,3]{1,0,2:T(1,128)} %param.13) | copy-start | bytes 2308
  10.1 29.3 %all-to-all-start = ((bf16[32,64,128]{2,1,0:T(8,128)(2,1)}), bf16[32,64,128]{2,1,0:T(8,128)(2,1)}, u32[]{:S(2)}, u32[]{:S(2)}) async-start(bf16[32,64,128]{2,1,0:T(8,128)(2,1)} %bitcast.1), calls=%async_computation | async-start | bytes 1048576 | tf_op jit(solution)/shard_map/all_to_all | solution.py:64
  21.8 25.3 %copy-start.25 = (s32[1,128]{1,0:T(1,128)S(1)}, s32[1,128]{1,0:T(1,128)}, u32[]{:S(2)}) copy-start(s32[1,128]{1,0:T(1,128)} %param.14) | copy-start | bytes 1540
  39.4 21.6 %all-to-all-start.4 = ((bf16[32,64,128]{2,1,0:T(8,128)(2,1)}), bf16[32,64,128]{2,1,0:T(8,128)(2,1)S(1)}, u32[]{:S(2)}, u32[]{:S(2)}) async-start(bf16[32,64,128]{2,1,0:T(8,128)(2,1)} %bitcast.34), calls=%async_computation.4 | async-start | bytes 1048576 | tf_op jit(solution)/shard_map/all_to_all | solution.py:64
  61.0 21.5 %all-to-all-start.1 = ((bf16[32,64,128]{2,1,0:T(8,128)(2,1)}), bf16[32,64,128]{2,1,0:T(8,128)(2,1)S(1)}, u32[]{:S(2)}, u32[]{:S(2)}) async-start(bf16[32,64,128]{2,1,0:T(8,128)(2,1)} %bitcast.361), calls=%async_computation.1 | async-start | bytes 1048576 | tf_op jit(solution)/shard_map/all_to_all | solution.py:64
  66.4 19.3 %collective-permute-start.1 = (bf16[32,64,128]{2,1,0:T(8,128)(2,1)S(1)}, bf16[32,64,128]{2,1,0:T(8,128)(2,1)}, u32[]{:S(2)}, u32[]{:S(2)}) collective-permute-start(bf16[32,64,128]{2,1,0:T(8,128)(2,1)S(1)} %all-to-all-done.4), channel_id=1, source_target_pairs={{0,8},{8,0},{16,24},{24,16},{1,9},{9,1},{17,25},{25,17},{2,10},{10... | collective-permute-start | bytes 1572872 | tf_op jit(solution)/shard_map/ppermute | solution.py:58
  68.3 27.3 %collective-permute-start = (bf16[32,64,128]{2,1,0:T(8,128)(2,1)}, bf16[32,64,128]{2,1,0:T(8,128)(2,1)}, u32[]{:S(2)}, u32[]{:S(2)}) collective-permute-start(bf16[32,64,128]{2,1,0:T(8,128)(2,1)} %all-to-all-done), channel_id=1, source_target_pairs={{0,8},{8,0},{16,24},{24,16},{1,9},{9,1},{17,25},{25,17},{2,10},{10... | collective-permute-start | bytes 1572872 | tf_op jit(solution)/shard_map/ppermute | solution.py:58
  146.2 13.9 %all-to-all-start.9 = ((bf16[1,32,64,128]{3,2,0,1:T(8,128)(2,1)}), bf16[1,32,64,128]{3,2,0,1:T(8,128)(2,1)}, u32[]{:S(2)}, u32[]{:S(2)}) async-start(bf16[1,32,64,128]{3,2,0,1:T(8,128)(2,1)} %all_to_all.71), calls=%async_computation.9 | async-start | bytes 1048576 | tf_op jit(solution)/shard_map/all_to_all | solution.py:136
  160.1 14.5 %all-to-all-start.2 = ((bf16[8,4,64,128]{3,2,1,0:T(8,128)(2,1)}), bf16[8,4,64,128]{3,2,1,0:T(8,128)(2,1)}, u32[]{:S(2)}, u32[]{:S(2)}) async-start(bf16[8,4,64,128]{3,2,1,0:T(8,128)(2,1)} %bitcast.29), calls=%async_computation.2 | async-start | bytes 1048576 | tf_op jit(solution)/shard_map/all_to_all | solution.py:183
  174.6 35.9 %all-to-all-start.3 = ((bf16[1,32,64,128]{3,2,0,1:T(8,128)(2,1)}), bf16[1,32,64,128]{3,2,0,1:T(8,128)(2,1)}, u32[]{:S(2)}, u32[]{:S(2)}) async-start(bf16[1,32,64,128]{3,2,0,1:T(8,128)(2,1)} %bitcast.31), calls=%async_computation.3 | async-start | bytes 1048576 | tf_op jit(solution)/shard_map/all_to_all | solution.py:182
  210.5 28.9 %all-to-all-start.10 = ((bf16[4,8,8,4096]{3,2,1,0:T(8,128)(2,1)}), bf16[4,8,8,4096]{3,2,1,0:T(8,128)(2,1)}, u32[]{:S(2)}, u32[]{:S(2)}) async-start(bf16[4,8,8,4096]{3,2,1,0:T(8,128)(2,1)} %bitcast.331), calls=%async_computation.10 | async-start | bytes 4194304 | tf_op jit(solution)/shard_map/all_to_all | solution.py:166
  235.2 12.4 %copy-start.17 = (bf16[128,4096]{1,0:T(8,128)(2,1)}, bf16[128,4096]{1,0:T(8,128)(2,1)S(1)}, u32[]{:S(2)}) copy-start(bf16[128,4096]{1,0:T(8,128)(2,1)S(1)} %multiply_convert_fusion.1) | copy-start | bytes 3145732
  242.3 21.2 %all-to-all-start.11 = ((bf16[8,8,4096]{2,1,0:T(8,128)(2,1)}), bf16[8,8,4096]{2,1,0:T(8,128)(2,1)}, u32[]{:S(2)}, u32[]{:S(2)}) async-start(bf16[8,8,4096]{2,1,0:T(8,128)(2,1)} %reduce_sum.64), calls=%async_computation.11 | async-start | bytes 1048576 | tf_op jit(solution)/shard_map/all_to_all | solution.py:176
  257.5 12.4 %copy-start.18 = (bf16[128,4096]{1,0:T(8,128)(2,1)S(1)}, bf16[128,4096]{1,0:T(8,128)(2,1)}, u32[]{:S(2)}) copy-start(bf16[128,4096]{1,0:T(8,128)(2,1)} %copy-done.17) | copy-start | bytes 3145732
  263.4 59.9 %all-to-all-start.5 = ((bf16[32,64,128]{2,1,0:T(8,128)(2,1)}), bf16[32,64,128]{2,1,0:T(8,128)(2,1)}, u32[]{:S(2)}, u32[]{:S(2)}) async-start(bf16[32,64,128]{2,1,0:T(8,128)(2,1)} %bitcast.360), calls=%async_computation.5 | async-start | bytes 1048576 | tf_op jit(solution)/shard_map/all_to_all | solution.py:307
  268.1 110.6 %all-gather.5.cloned.1.call-start = ((), (), s32[]{:S(2)}) async-start(), calls=%async_computation.13 | async-start | bytes 2162688 | tf_op jit(solution)/shard_map/all_gather | solution.py:181
  282.4 39.9 %collective-permute-start.2 = (bf16[32,64,128]{2,1,0:T(8,128)(2,1)S(1)}, bf16[32,64,128]{2,1,0:T(8,128)(2,1)S(1)}, u32[]{:S(2)}, u32[]{:S(2)}) collective-permute-start(bf16[32,64,128]{2,1,0:T(8,128)(2,1)S(1)} %fusion.49), channel_id=1, source_target_pairs={{0,8},{8,0},{16,24},{24,16},{1,9},{9,1},{17,25},{25,17},{2,10},{10... | collective-permute-start | bytes 1572872 | tf_op jit(solution)/shard_map/ppermute | solution.py:303
  323.3 29.0 %copy-start.16 = (f32[4096,128]{1,0:T(8,128)S(1)}, f32[4096,128]{1,0:T(8,128)}, u32[]{:S(2)}) copy-start(f32[4096,128]{1,0:T(8,128)} %scatter_fusion.1) | copy-start | bytes 6291460
  323.3 30.1 %all-to-all-start.6 = ((bf16[32,64,128]{2,1,0:T(8,128)(2,1)}), bf16[32,64,128]{2,1,0:T(8,128)(2,1)S(1)}, u32[]{:S(2)}, u32[]{:S(2)}) async-start(bf16[32,64,128]{2,1,0:T(8,128)(2,1)} %fusion.48), calls=%async_computation.6 | async-start | bytes 1048576 | tf_op jit(solution)/shard_map/all_to_all | solution.py:307
  334.4 18.0 %collective-permute-start.3 = (bf16[32,64,128]{2,1,0:T(8,128)(2,1)S(1)}, bf16[32,64,128]{2,1,0:T(8,128)(2,1)S(1)}, u32[]{:S(2)}, u32[]{:S(2)}) collective-permute-start(bf16[32,64,128]{2,1,0:T(8,128)(2,1)S(1)} %fusion.50), channel_id=1, source_target_pairs={{0,8},{8,0},{16,24},{24,16},{1,9},{9,1},{17,25},{25,17},{2,10},{10... | collective-permute-start | bytes 1572872 | tf_op jit(solution)/shard_map/ppermute | solution.py:303
  353.4 23.9 %all-to-all-start.7 = ((bf16[32,64,128]{2,1,0:T(8,128)(2,1)}), bf16[32,64,128]{2,1,0:T(8,128)(2,1)S(1)}, u32[]{:S(2)}, u32[]{:S(2)}) async-start(bf16[32,64,128]{2,1,0:T(8,128)(2,1)} %fusion.47), calls=%async_computation.7 | async-start | bytes 1048576 | tf_op jit(solution)/shard_map/all_to_all | solution.py:307
  (20 other events, 91.2 us)
Sparse Core Ops, SparseCore 0:
  9.9 54.2 all-gather.2
  271.5 81.7 all-gather.4
where the time goes:
time: 395 us; the launch traced here: 389 us
  waiting for transfers between devices  111 us (28%)
  starting transfers between devices  86.8 us (22%)
  matrix products  65 us (16%)
  local copies, waits for them, and re-layouts  55.1 us (14%)
  other arithmetic  30.4 us (8%)
  blocking collectives  25.7 us (7%)
  between operations  15.1 us (4%)
    all_to_all x3, waiting for transfers between devices, to_heads(): lax.all_to_all(head_rows(rows), SEQ_AXES, split_axis=0, concat_axis=0, ti...  43.4 us
    all_to_all x1, blocking collectives, shards(): lax.all_to_all(attention.reshape(1, seq_devices, slice_rows, columns), SE...  25.7 us
    all_to_all x3, starting transfers between devices, to_positions(): lax.all_to_all(rows, SEQ_AXES, split_axis=0, concat_axis=0, tiled=True)  21.4 us
    all_to_all x3, starting transfers between devices, to_heads(): lax.all_to_all(head_rows(rows), SEQ_AXES, split_axis=0, concat_axis=0, ti...  20.8 us
    all_to_all x1, starting transfers between devices, shards(): lax.all_to_all(lax.all_to_all(delta_blocks, DP_AXES, split_axis=0, concat...  18.6 us
    dot_general x2, matrix products, place_blocks(): jnp.einsum('bjc,bjke->cke', block_hot, parts.reshape(query_blocks, 3 + RA...  16.2 us
    ppermute x2, waiting for transfers between devices, my_half(): received = lax.ppermute(theirs.astype(jnp.bfloat16), 'sx', partner)  16.1 us
    all_to_all x3, waiting for transfers between devices, to_positions(): lax.all_to_all(rows, SEQ_AXES, split_axis=0, concat_axis=0, tiled=True)  12.7 us
  transfers between devices with their start and end apart: 17, of which 12 were waited for; matrix products, arithmetic and copies ran while one was open for 36% of the time, Pallas kernels for 0%

commit v1 on v0

--- a/solution.py
+++ b/solution.py
@@ -58,14 +58,17 @@
         other = lax.ppermute(mine, "sx", partner)
         low = jnp.where(my_slice == 0, mine, other)
         high = jnp.where(my_slice == 0, other, mine)
-        return jnp.stack([low, high], axis=1).reshape(seq_devices, tokens, columns)
-
-    def to_heads(rows):
-        return lax.all_to_all(head_rows(rows), SEQ_AXES, split_axis=0, concat_axis=0, tiled=True)
-
-    query_head = to_heads(query_rows)
-    key_head = both_halves(to_heads(key_rows))
-    value_head = both_halves(to_heads(value_rows))
+        return jnp.stack([low, high], axis=2).reshape(mine.shape[0], seq_devices, tokens, columns)
+
+    head_parts = lax.all_to_all(
+        jnp.stack([head_rows(query_rows), head_rows(key_rows), head_rows(value_rows)], axis=0),
+        SEQ_AXES,
+        split_axis=1,
+        concat_axis=1,
+        tiled=True,
+    )
+    query_head = head_parts[0]
+    key_head, value_head = both_halves(head_parts[1:])
     source_start = jnp.arange(seq_devices, dtype=jnp.int32)[:, None] * tokens
     offsets = jnp.arange(slice_rows, dtype=jnp.int32)[None, :]
     query_pos = (source_start + my_slice * slice_rows + offsets).reshape(query_count)
@@ -296,26 +299,32 @@
     grad_query_all = grad_query.reshape(query_count, columns) + jnp.dot(
         picker_f, grad_query_glob, precision=lax.Precision.HIGHEST
     )
-    def my_half(grads):
-        halves = grads.reshape(seq_devices, splitting, slice_rows, columns)
-        mine = jnp.where(my_slice == 0, halves[:, 0], halves[:, 1])
-        theirs = jnp.where(my_slice == 0, halves[:, 1], halves[:, 0])
-        received = lax.ppermute(theirs.astype(jnp.bfloat16), "sx", partner)
-        return (mine + received.astype(jnp.float32)).astype(jnp.bfloat16)
-
-    def to_positions(rows):
-        back = lax.all_to_all(rows, SEQ_AXES, split_axis=0, concat_axis=0, tiled=True)
-        return (
-            back.reshape(head_groups, splitting, slice_rows, columns)
-            .transpose(1, 2, 0, 3)
-            .reshape(1, tokens, width)
-        )
-
-    grad_queries = to_positions(
-        grad_query_all.astype(jnp.bfloat16).reshape(seq_devices, slice_rows, columns)
-    )
-    grad_keys = to_positions(my_half(grad_key))
-    grad_values = to_positions(my_half(grad_value))
+    halves = jnp.stack([grad_key, grad_value], axis=0).reshape(
+        2, seq_devices, splitting, slice_rows, columns
+    )
+    mine = jnp.where(my_slice == 0, halves[:, :, 0], halves[:, :, 1])
+    theirs = jnp.where(my_slice == 0, halves[:, :, 1], halves[:, :, 0])
+    received = lax.ppermute(theirs.astype(jnp.bfloat16), "sx", partner)
+    pair_sums = (mine + received.astype(jnp.float32)).astype(jnp.bfloat16)
+    back = lax.all_to_all(
+        jnp.concatenate(
+            [
+                grad_query_all.astype(jnp.bfloat16).reshape(1, seq_devices, slice_rows, columns),
+                pair_sums,
+            ],
+            axis=0,
+        ),
+        SEQ_AXES,
+        split_axis=1,
+        concat_axis=1,
+        tiled=True,
+    )
+    back = (
+        back.reshape(3, head_groups, splitting, slice_rows, columns)
+        .transpose(0, 2, 3, 1, 4)
+        .reshape(3, 1, tokens, width)
+    )
+    grad_queries, grad_keys, grad_values = back[0], back[1], back[2]
     return (grad_queries, grad_keys, grad_values, grad_out_proj)
 
 

time: 395 us -> 402 us (1.018)
  blocking collectives: 25.7 us -> 75.4 us
  starting transfers between devices: 86.8 us -> 50.5 us
  waiting for transfers between devices: 111 us -> 96.3 us
  matrix products: 65 us -> 71.7 us
    all_to_all x0 -> x1, blocking collectives: none -> 52.9 us  [shards(): lax.all_to_all(jnp.concatenate([grad_query_all.astype(jnp.bfloat16).resha...]
    all_to_all x6 -> x1, starting transfers between devices: 42.1 us -> 11.6 us  [shards(): lax.all_to_all(jnp.stack([head_rows(query_rows), head_rows(key_rows), hea...]
    all_to_all x6 -> x1, waiting for transfers between devices: 56.1 us -> 37.2 us  [shards(): lax.all_to_all(jnp.stack([head_rows(query_rows), head_rows(key_rows), hea...]
    all_to_all x1, starting transfers between devices: 18.6 us -> 4.67 us  [shards(): lax.all_to_all(lax.all_to_all(delta_blocks, DP_AXES, split_axis=0, concat...]
    all_to_all x1, starting transfers between devices: 4.92 us -> 16.9 us  [shards(): lax.all_to_all(lax.all_to_all(attention.reshape(1, seq_devices, slice_row...]
    ppermute x2 -> x1, waiting for transfers between devices: 10.3 us -> 19.9 us  [both_halves(): other = lax.ppermute(mine, 'sx', partner)]
    mul x0 -> x1, local copies, waits for them, and re-layouts: none -> 6.62 us  [shards(): jnp.einsum('bhqk,bqhe->bkhe', score_bf[..., :window_keys], query_blk, pre...]
    all_gather x1, waiting for transfers between devices: 0.01 us -> 4.87 us  [shards(): lax.all_gather(z_sum.astype(jnp.bfloat16), SEQ_AXES, axis=0, tiled=True)]
  transfers between devices with their start and end apart: 17 -> 10, of which waited for: 12 -> 7; matrix products, arithmetic and copies ran while one was open for 36% -> 38% of each run, Pallas kernels for 0% -> 0%
where the time goes in v1:
time: 402 us; the launch traced here: 398 us
  waiting for transfers between devices  96.3 us (24%)
  blocking collectives  75.4 us (19%)
  matrix products  71.7 us (18%)
  local copies, waits for them, and re-layouts  57 us (14%)
  starting transfers between devices  50.5 us (13%)
  other arithmetic  32.1 us (8%)
  between operations  14.9 us (4%)
    all_to_all x1, blocking collectives, shards(): lax.all_to_all(jnp.concatenate([grad_query_all.astype(jnp.bfloat16).resha...  52.9 us
    all_to_all x1, waiting for transfers between devices, shards(): lax.all_to_all(jnp.stack([head_rows(query_rows), head_rows(key_rows), hea...  37.2 us
    all_to_all x1, blocking collectives, shards(): lax.all_to_all(attention.reshape(1, seq_devices, slice_rows, columns), SE...  22.5 us
    ppermute x1, waiting for transfers between devices, both_halves(): other = lax.ppermute(mine, 'sx', partner)  19.9 us
    dot_general x2, matrix products, place_blocks(): jnp.einsum('bjc,bjke->cke', block_hot, parts.reshape(query_blocks, 3 + RA...  17.4 us
    all_to_all x1, starting transfers between devices, shards(): lax.all_to_all(lax.all_to_all(attention.reshape(1, seq_devices, slice_row...  16.9 us
    ppermute x1, waiting for transfers between devices, shards(): received = lax.ppermute(theirs.astype(jnp.bfloat16), 'sx', partner)  14.1 us
    all_to_all x1, starting transfers between devices, shards(): lax.all_to_all(jnp.stack([head_rows(query_rows), head_rows(key_rows), hea...  11.6 us
  transfers between devices with their start and end apart: 10, of which 7 were waited for; matrix products, arithmetic and copies ran while one was open for 38% of the time, Pallas kernels for 0%

profile of v1, /device:TPU:8, one launch (start us, length us, event | category | flops | bytes accessed | tf_op | source)
XLA Modules:
  0.0 397.9 jit_solution(11566853606837194229)
XLA Ops:
  11.2 11.6 %all-to-all-start = ((bf16[3,32,64,128]{3,2,0,1:T(8,128)(2,1)}), bf16[3,32,64,128]{3,2,0,1:T(8,128)(2,1)}, u32[]{:S(2)}, u32[]{:S(2)}) async-start(bf16[3,32,64,128]{3,2,0,1:T(8,128)(2,1)} %pad_maximum_fusion.2), calls=%async_computation | async-start | bytes 3145728 | tf_op jit(solution)/shard_map/all_to_all | solution.py:63
  24.6 37.2 %all-to-all-done = bf16[3,32,64,128]{3,2,0,1:T(8,128)(2,1)} async-done(((bf16[3,32,64,128]{3,2,0,1:T(8,128)(2,1)}), bf16[3,32,64,128]{3,2,0,1:T(8,128)(2,1)}, u32[]{:S(2)}, u32[]{:S(2)}) %all-to-all-start) | async-done | bytes 1572896 | tf_op jit(solution)/shard_map/all_to_all | solution.py:63
  67.9 19.9 %collective-permute-done = bf16[2,32,64,128]{3,2,1,0:T(8,128)(2,1)S(1)} collective-permute-done((bf16[2,32,64,128]{3,2,1,0:T(8,128)(2,1)}, bf16[2,32,64,128]{3,2,1,0:T(8,128)(2,1)S(1)}, u32[]{:S(2)}, u32[]{:S(2)}) %collective-permute-start) | collective-permute-done | bytes 1048608 | tf_op jit(solution)/shard_map/ppermute | solution.py:58
  101.9 4.0 %fusion.11 = (f32[32,64]{1,0:T(8,128)S(1)}, f32[32,1,64,384]{3,2,0,1:T(8,128)S(1)}) fusion(pred[32,384]{1,0:T(8,128)(4,1)S(1)} %concatenate.88, bf16[32,384,128]{2,1,0:T(8,128)(2,1)} %bitcast.319, bf16[3,32,64,128]{3,2,0,1:T(8,128)(2,1)} %all-to-all-done), kind=kOutput, calls=%fused_computation.30 | convolution fusion | flops 203683840 | bytes 6836224 | tf_op jit(solution)/shard_map/bqhe,bkhe->bhqk/dot_general | solution.py:97
  115.4 22.5 %all_to_all.51 = bf16[1,32,64,128]{3,2,0,1:T(8,128)(2,1)} all-to-all(bf16[1,32,64,128]{3,2,0,1:T(8,128)(2,1)S(1)} %bitcast.354), channel_id=1, replica_groups=mesh['sz'=8,'sx'=4,'dy'=4,'dc'=2] {'sz','sx'}, dimensions={1} | all-to-all | bytes 1048576 | tf_op jit(solution)/shard_map/all_to_all | solution.py:140
  137.9 16.9 %all-to-all-start.5 = ((bf16[1,32,64,128]{3,2,0,1:T(8,128)(2,1)}), bf16[1,32,64,128]{3,2,0,1:T(8,128)(2,1)}, u32[]{:S(2)}, u32[]{:S(2)}) async-start(bf16[1,32,64,128]{3,2,0,1:T(8,128)(2,1)} %all_to_all.51), calls=%async_computation.5 | async-start | bytes 1048576 | tf_op jit(solution)/shard_map/all_to_all | solution.py:139
  154.8 4.9 %fusion.39 = bf16[8,2,2,64,128]{4,3,2,0,1:T(8,128)(2,1)S(1)} fusion(bf16[2,128,4096,1,1]{2,1,4,3,0:T(8,128)(2,1)S(1)} %bitcast.314, bf16[8,2,64,4096,1]{3,2,1,0,4:T(8,128)(2,1)} %bitcast.333), kind=kOutput, calls=%fused_computation.78 | convolution fusion | flops 2147745792 | bytes 11010048 | tf_op jit(solution)/shard_map/kptd,gcd->kgptc/dot_general | solution.py:157
  163.8 5.5 %all-to-all-start.1 = ((bf16[8,4,64,128]{3,2,1,0:T(8,128)(2,1)}), bf16[8,4,64,128]{3,2,1,0:T(8,128)(2,1)}, u32[]{:S(2)}, u32[]{:S(2)}) async-start(bf16[8,4,64,128]{3,2,1,0:T(8,128)(2,1)} %bitcast.31), calls=%async_computation.1 | async-start | bytes 1048576 | tf_op jit(solution)/shard_map/all_to_all | solution.py:186
  172.0 6.3 %all-to-all-done.1 = bf16[8,4,64,128]{3,2,1,0:T(8,128)(2,1)} async-done(((bf16[8,4,64,128]{3,2,1,0:T(8,128)(2,1)}), bf16[8,4,64,128]{3,2,1,0:T(8,128)(2,1)}, u32[]{:S(2)}, u32[]{:S(2)}) %all-to-all-start.1) | async-done | bytes 524320 | tf_op jit(solution)/shard_map/all_to_all | solution.py:186
  178.3 4.7 %all-to-all-start.2 = ((bf16[1,32,64,128]{3,2,0,1:T(8,128)(2,1)}), bf16[1,32,64,128]{3,2,0,1:T(8,128)(2,1)}, u32[]{:S(2)}, u32[]{:S(2)}) async-start(bf16[1,32,64,128]{3,2,0,1:T(8,128)(2,1)} %bitcast.33), calls=%async_computation.2 | async-start | bytes 1048576 | tf_op jit(solution)/shard_map/all_to_all | solution.py:185
  183.0 5.9 %fusion.4 = bf16[256,4096]{1,0:T(8,128)(2,1)S(1)} fusion(bf16[256,8,2,64]{0,3,2,1:T(8,128)(2,1)} %dot_general.135, bf16[8,2,64,4096]{3,2,1,0:T(8,128)(2,1)} %bitcast.334), kind=kOutput, calls=%fused_computation.13 | convolution fusion | flops 2148532224 | bytes 11010048 | tf_op jit(solution)/shard_map/kgptc,kptd->gcd/dot_general | solution.py:162
  190.5 10.0 %all-to-all-done.2 = bf16[1,32,64,128]{3,2,0,1:T(8,128)(2,1)} async-done(((bf16[1,32,64,128]{3,2,0,1:T(8,128)(2,1)}), bf16[1,32,64,128]{3,2,0,1:T(8,128)(2,1)}, u32[]{:S(2)}, u32[]{:S(2)}) %all-to-all-start.2) | async-done | bytes 524320 | tf_op jit(solution)/shard_map/all_to_all | solution.py:185
  200.6 4.6 %all-to-all-start.6 = ((bf16[4,8,8,4096]{3,2,1,0:T(8,128)(2,1)}), bf16[4,8,8,4096]{3,2,1,0:T(8,128)(2,1)}, u32[]{:S(2)}, u32[]{:S(2)}) async-start(bf16[4,8,8,4096]{3,2,1,0:T(8,128)(2,1)} %bitcast.335), calls=%async_computation.6 | async-start | bytes 4194304 | tf_op jit(solution)/shard_map/all_to_all | solution.py:169
  220.6 5.2 %multiply_bitcast_fusion = f32[32,384,1,128]{1,3,0,2:T(8,128)} fusion(bf16[32,1,64,512]{3,2,0,1:T(8,128)(2,1)} %multiply_convert_fusion, bf16[3,32,64,128]{3,2,0,1:T(8,128)(2,1)} %all-to-all-done), kind=kOutput, calls=%fused_computation.11 | convolution fusion | flops 202899456 | bytes 8388608 | tf_op jit(solution)/shard_map/bhqk,bqhe->bkhe/dot_general | solution.py:221
  225.8 6.6 %copy.135 = f32[32,384,1,128]{3,1,0,2:T(8,128)} copy(f32[32,384,1,128]{1,3,0,2:T(8,128)} %multiply_bitcast_fusion) | data formatting | bytes 12582912 | tf_op jit(solution)/shard_map/mul | solution.py:221
  232.4 8.7 %fusion.25 = f32[64,64,128]{2,0,1:T(8,128)S(1)} fusion(f32[32,6,64,128]{3,2,1,0:T(8,128)} %bitcast.324, s32[32,6]{0,1:T(8,128)S(1)} %pad_add_fusion), kind=kOutput, calls=%fused_computation.58 | convolution fusion | flops 1207971840 | bytes 8389376 | tf_op jit(solution)/shard_map/bjc,bjke->cke/dot_general | solution.py:255
  244.6 5.2 %convolution_bitcast_fusion.2 = f32[32,384,1,128]{1,3,0,2:T(8,128)} fusion(bf16[32,1,64,512]{3,2,0,1:T(8,128)(2,1)} %get-tuple-element.7, bf16[1,32,64,128]{3,2,0,1:T(8,128)(2,1)} %all-to-all-done.2), kind=kOutput, calls=%fused_computation.32 | convolution fusion | flops 201326592 | bytes 8388608 | tf_op jit(solution)/shard_map/bhqk,bqhe->bkhe/dot_general | solution.py:238
  249.9 6.6 %copy.141 = f32[32,384,1,128]{3,1,0,2:T(8,128)} copy(f32[32,384,1,128]{1,3,0,2:T(8,128)} %convolution_bitcast_fusion.2) | data formatting | bytes 12582912 | tf_op jit(solution)/shard_map/bhqk,bqhe->bkhe/transpose | solution.py:238
  256.5 8.7 %fusion.28 = f32[64,64,128]{2,0,1:T(8,128)S(1)} fusion(f32[32,6,64,128]{3,2,1,0:T(8,128)} %bitcast.323, s32[32,6]{0,1:T(8,128)S(1)} %pad_add_fusion), kind=kOutput, calls=%fused_computation.59 | convolution fusion | flops 1207971840 | bytes 8389376 | tf_op jit(solution)/shard_map/bjc,bjke->cke/dot_general | solution.py:255
  280.8 4.1 %all-to-all-start.7 = ((bf16[8,8,4096]{2,1,0:T(8,128)(2,1)}), bf16[8,8,4096]{2,1,0:T(8,128)(2,1)}, u32[]{:S(2)}, u32[]{:S(2)}) async-start(bf16[8,8,4096]{2,1,0:T(8,128)(2,1)} %reduce_sum.64), calls=%async_computation.7 | async-start | bytes 1048576 | tf_op jit(solution)/shard_map/all_to_all | solution.py:179
  290.6 4.1 %scatter_fusion = f32[4096,128]{1,0:T(8,128)} fusion(f32[4096,128]{1,0:T(8,128)} %copy.139, s32[128]{0:T(128)S(1)} %fusion.83, f32[128,128]{1,0:T(8,128)S(1)} %copy.140), kind=kCustom, calls=%fused_computation.5 | custom fusion | flops 16384 | bytes 197120 | tf_op jit(solution)/shard_map/scatter-add | solution.py:264
  309.4 14.1 %collective-permute-done.1 = bf16[2,32,64,128]{3,2,1,0:T(8,128)(2,1)} collective-permute-done((bf16[2,32,64,128]{3,2,1,0:T(8,128)(2,1)}, bf16[2,32,64,128]{3,2,1,0:T(8,128)(2,1)}, u32[]{:S(2)}, u32[]{:S(2)}) %collective-permute-start.1) | collective-permute-done | bytes 1048608 | tf_op jit(solution)/shard_map/ppermute | solution.py:307
  325.7 52.9 %all_to_all.52 = bf16[3,32,64,128]{3,2,0,1:T(8,128)(2,1)S(1)} all-to-all(bf16[3,32,64,128]{3,2,0,1:T(8,128)(2,1)S(1)} %copy.147), channel_id=1, replica_groups=mesh['sz'=8,'sx'=4,'dy'=4,'dc'=2] {'sz','sx'}, dimensions={1} | all-to-all | bytes 3145728 | tf_op jit(solution)/shard_map/all_to_all | solution.py:309
  382.8 4.9 %all-gather.5.cloned.1.call-done = bf16[256,4096]{1,0:T(8,128)(2,1)} async-done(((bf16[8,4096]{1,0:T(8,128)(2,1)}), bf16[256,4096]{1,0:T(8,128)(2,1)}) %all-gather.5.cloned.1.call-update) | async-done | bytes 2097168 | tf_op jit(solution)/shard_map/all_gather | solution.py:184
  (155 shorter events, 107.8 us)
Async XLA Ops:
  7.2 147.7 %copy-start = (bf16[256,4096]{1,0:T(8,128)(2,1)S(1)}, bf16[256,4096]{1,0:T(8,128)(2,1)}, u32[]{:S(2)}) copy-start(bf16[256,4096]{1,0:T(8,128)(2,1)} %param.15) | copy-start | bytes 6291460
  7.2 147.6 %all-gather.3.cloned.1.call-start = ((), (), s32[]{:S(2)}) async-start(), calls=%async_computation.8 | async-start | bytes 9437184 | tf_op jit(solution)/shard_map/all_gather | solution.py:154
  11.2 11.7 %copy-start.22 = (s32[1,64,3]{1,0,2:T(1,128)S(1)}, s32[1,64,3]{1,0,2:T(1,128)}, u32[]{:S(2)}) copy-start(s32[1,64,3]{1,0,2:T(1,128)} %param.13) | copy-start | bytes 2308
  11.2 12.7 %copy-start.21 = (s32[1,128]{1,0:T(1,128)S(1)}, s32[1,128]{1,0:T(1,128)}, u32[]{:S(2)}) copy-start(s32[1,128]{1,0:T(1,128)} %param.14) | copy-start | bytes 1540
  11.2 50.7 %all-to-all-start = ((bf16[3,32,64,128]{3,2,0,1:T(8,128)(2,1)}), bf16[3,32,64,128]{3,2,0,1:T(8,128)(2,1)}, u32[]{:S(2)}, u32[]{:S(2)}) async-start(bf16[3,32,64,128]{3,2,0,1:T(8,128)(2,1)} %pad_maximum_fusion.2), calls=%async_computation | async-start | bytes 3145728 | tf_op jit(solution)/shard_map/all_to_all | solution.py:63
  64.2 23.6 %collective-permute-start = (bf16[2,32,64,128]{3,2,1,0:T(8,128)(2,1)}, bf16[2,32,64,128]{3,2,1,0:T(8,128)(2,1)S(1)}, u32[]{:S(2)}, u32[]{:S(2)}) collective-permute-start(bf16[2,32,64,128]{3,2,1,0:T(8,128)(2,1)} %copy.159), channel_id=1, source_target_pairs={{0,8},{8,0},{16,24},{24,16},{1,9},{9,1},{17,25},{25,17},{2,10},{10... | collective-permute-start | bytes 3145736 | tf_op jit(solution)/shard_map/ppermute | solution.py:58
  101.9 6.2 %copy-start.7 = (f32[32,1,64,128]{3,2,0,1:T(8,128)}, f32[32,1,64,128]{3,2,0,1:T(8,128)S(1)}, u32[]{:S(2)}) copy-start(f32[32,1,64,128]{3,2,0,1:T(8,128)S(1)} %get-tuple-element.23) | copy-start | bytes 3145732
  106.5 5.3 %copy-start.12 = (f32[128,4096]{1,0:T(8,128)}, f32[128,4096]{1,0:T(8,128)S(1)}, u32[]{:S(2)}) copy-start(f32[128,4096]{1,0:T(8,128)S(1)} %get-tuple-element.25) | copy-start | bytes 6291460
  137.9 25.9 %all-to-all-start.5 = ((bf16[1,32,64,128]{3,2,0,1:T(8,128)(2,1)}), bf16[1,32,64,128]{3,2,0,1:T(8,128)(2,1)}, u32[]{:S(2)}, u32[]{:S(2)}) async-start(bf16[1,32,64,128]{3,2,0,1:T(8,128)(2,1)} %all_to_all.51), calls=%async_computation.5 | async-start | bytes 1048576 | tf_op jit(solution)/shard_map/all_to_all | solution.py:139
  163.8 14.5 %all-to-all-start.1 = ((bf16[8,4,64,128]{3,2,1,0:T(8,128)(2,1)}), bf16[8,4,64,128]{3,2,1,0:T(8,128)(2,1)}, u32[]{:S(2)}, u32[]{:S(2)}) async-start(bf16[8,4,64,128]{3,2,1,0:T(8,128)(2,1)} %bitcast.31), calls=%async_computation.1 | async-start | bytes 1048576 | tf_op jit(solution)/shard_map/all_to_all | solution.py:186
  178.3 22.3 %all-to-all-start.2 = ((bf16[1,32,64,128]{3,2,0,1:T(8,128)(2,1)}), bf16[1,32,64,128]{3,2,0,1:T(8,128)(2,1)}, u32[]{:S(2)}, u32[]{:S(2)}) async-start(bf16[1,32,64,128]{3,2,0,1:T(8,128)(2,1)} %bitcast.33), calls=%async_computation.2 | async-start | bytes 1048576 | tf_op jit(solution)/shard_map/all_to_all | solution.py:185
  200.6 6.4 %copy-start.11 = (bf16[1,32,2,64,128]{4,3,2,1,0:T(8,128)(2,1)S(1)}, bf16[1,32,2,64,128]{4,3,2,1,0:T(8,128)(2,1)}, u32[]{:S(2)}) copy-start(bf16[1,32,2,64,128]{4,3,2,1,0:T(8,128)(2,1)} %get-tuple-element.13) | copy-start | bytes 3145732
  200.6 77.3 %all-to-all-start.6 = ((bf16[4,8,8,4096]{3,2,1,0:T(8,128)(2,1)}), bf16[4,8,8,4096]{3,2,1,0:T(8,128)(2,1)}, u32[]{:S(2)}, u32[]{:S(2)}) async-start(bf16[4,8,8,4096]{3,2,1,0:T(8,128)(2,1)} %bitcast.335), calls=%async_computation.6 | async-start | bytes 4194304 | tf_op jit(solution)/shard_map/all_to_all | solution.py:169
  206.9 5.0 %copy-start.6 = (bf16[192,64,128]{2,1,0:T(8,128)(2,1)S(1)}, bf16[192,64,128]{2,1,0:T(8,128)(2,1)}, u32[]{:S(2)}) copy-start(bf16[192,64,128]{2,1,0:T(8,128)(2,1)} %gather_fusion.2) | copy-start | bytes 9437188
  211.9 2.7 copy-start.3
  267.7 3.0 copy-start.13
  277.8 8.9 %copy-start.16 = (f32[4096,128]{0,1:T(8,128)S(1)}, f32[4096,128]{0,1:T(8,128)}, u32[]{:S(2)}) copy-start(f32[4096,128]{0,1:T(8,128)} %fusion.7) | copy-start | bytes 6291460
  280.8 22.9 %all-to-all-start.7 = ((bf16[8,8,4096]{2,1,0:T(8,128)(2,1)}), bf16[8,8,4096]{2,1,0:T(8,128)(2,1)}, u32[]{:S(2)}, u32[]{:S(2)}) async-start(bf16[8,8,4096]{2,1,0:T(8,128)(2,1)} %reduce_sum.64), calls=%async_computation.7 | async-start | bytes 1048576 | tf_op jit(solution)/shard_map/all_to_all | solution.py:179
  285.0 102.7 %all-gather.5.cloned.1.call-start = ((), (), s32[]{:S(2)}) async-start(), calls=%async_computation.9 | async-start | bytes 2162688 | tf_op jit(solution)/shard_map/all_gather | solution.py:184
  296.8 5.0 %copy-start.4 = (bf16[192,64,128]{2,1,0:T(8,128)(2,1)S(1)}, bf16[192,64,128]{2,1,0:T(8,128)(2,1)}, u32[]{:S(2)}) copy-start(bf16[192,64,128]{2,1,0:T(8,128)(2,1)} %gather_fusion.1) | copy-start | bytes 9437188
  296.8 5.0 %copy-start.14 = (bf16[32,1,64,512]{3,2,0,1:T(8,128)(2,1)S(1)}, bf16[32,1,64,512]{3,2,0,1:T(8,128)(2,1)}, u32[]{:S(2)}) copy-start(bf16[32,1,64,512]{3,2,0,1:T(8,128)(2,1)} %multiply_convert_fusion) | copy-start | bytes 6291460
  299.7 23.8 %collective-permute-start.1 = (bf16[2,32,64,128]{3,2,1,0:T(8,128)(2,1)}, bf16[2,32,64,128]{3,2,1,0:T(8,128)(2,1)}, u32[]{:S(2)}, u32[]{:S(2)}) collective-permute-start(bf16[2,32,64,128]{3,2,1,0:T(8,128)(2,1)} %fusion.49), channel_id=1, source_target_pairs={{0,8},{8,0},{16,24},{24,16},{1,9},{9,1},{17,25},{25,17},{2,10},{10... | collective-permute-start | bytes 3145736 | tf_op jit(solution)/shard_map/ppermute | solution.py:307
  305.5 18.0 %copy-start.9 = (f32[4096,128]{1,0:T(8,128)S(1)}, f32[4096,128]{1,0:T(8,128)}, u32[]{:S(2)}) copy-start(f32[4096,128]{1,0:T(8,128)} %scatter_fusion) | copy-start | bytes 6291460
  381.8 9.0 %copy-start.1 = (bf16[256,4096]{1,0:T(8,128)(2,1)S(1)}, bf16[256,4096]{1,0:T(8,128)(2,1)}, u32[]{:S(2)}) copy-start(bf16[256,4096]{1,0:T(8,128)(2,1)} %param.15) | copy-start | bytes 6291460
  (9 other events, 19.3 us)
Sparse Core Ops, SparseCore 0:
  9.9 54.3 all-gather.2
  305.7 81.9 all-gather.4

commit v2 on v0

--- a/solution.py
+++ b/solution.py
@@ -214,10 +214,11 @@
         )
     ) * scaling
     flat_ids = block_ids.reshape(-1)
+    window_blocks = (query_blocks, heads_here, BLOCK, 3 + RANDOM, BLOCK)
     key_part = (
         jnp.einsum(
-            "bhqk,bqhe->bkhe",
-            score_bf[..., :window_keys],
+            "bhqjk,bqhe->bjkhe",
+            score_bf[..., :window_keys].reshape(window_blocks),
             query_blk,
             preferred_element_type=jnp.float32,
         )
@@ -233,8 +234,8 @@
         * scaling
     )
     value_part = jnp.einsum(
-        "bhqk,bqhe->bkhe",
-        prob_kept[..., :window_keys],
+        "bhqjk,bqhe->bjkhe",
+        prob_kept[..., :window_keys].reshape(window_blocks),
         delta_blk,
         preferred_element_type=jnp.float32,
     )
@@ -253,7 +254,7 @@
             "bjc,bjke->cke",
             block_hot,
             parts.reshape(query_blocks, 3 + RANDOM, BLOCK, columns),
-            precision=lax.Precision.HIGHEST,
+            precision=lax.Precision.HIGH,
             preferred_element_type=jnp.float32,
         ).reshape(seq_length, columns)
 

time: 395 us -> 386 us (0.977)
  starting transfers between devices: 86.8 us -> 74.2 us
  waiting for transfers between devices: 111 us -> 121 us
  matrix products: 65 us -> 60.7 us
    all_to_all x1, starting transfers between devices: 18.6 us -> 4.8 us  [shards(): lax.all_to_all(lax.all_to_all(delta_blocks, DP_AXES, split_axis=0, concat...]
    all_to_all x1, waiting for transfers between devices: 4.31 us -> 12.4 us  [shards(): lax.all_to_all(x_sum.astype(jnp.bfloat16).reshape(z_size, z_rows, model_w...]
    transpose x1 -> x0, local copies, waits for them, and re-layouts: 6.58 us -> none  [shards(): jnp.einsum('bhqk,bqhe->bkhe', prob_kept[..., :window_keys], delta_blk, pr...]
    dot_general x2, matrix products: 16.2 us -> 10 us  [place_blocks(): jnp.einsum('bjc,bjke->cke', block_hot, parts.reshape(query_blocks, 3 + RA...]
    ppermute x2, waiting for transfers between devices: 16.1 us -> 20.5 us  [my_half(): received = lax.ppermute(theirs.astype(jnp.bfloat16), 'sx', partner)]
    all_to_all x1, waiting for transfers between devices: 4.18 us -> 0.01 us  [shards(): lax.all_to_all(proj_part.reshape(z_size, x_size, z_rows, model_width).tra...]
    unnamed x59 -> x57, local copies, waits for them, and re-layouts: 8.49 us -> 9.04 us
  transfers between devices with their start and end apart: 17 -> 17, of which waited for: 12 -> 11; matrix products, arithmetic and copies ran while one was open for 36% -> 36% of each run, Pallas kernels for 0% -> 0%
where the time goes in v2:
time: 386 us; the launch traced here: 381 us
  waiting for transfers between devices  121 us (31%)
  starting transfers between devices  74.2 us (19%)
  matrix products  60.7 us (16%)
  local copies, waits for them, and re-layouts  53.4 us (14%)
  other arithmetic  30.8 us (8%)
  blocking collectives  25.5 us (7%)
  between operations  15.1 us (4%)
    all_to_all x3, waiting for transfers between devices, to_heads(): lax.all_to_all(head_rows(rows), SEQ_AXES, split_axis=0, concat_axis=0, ti...  43.2 us
    all_to_all x1, blocking collectives, shards(): lax.all_to_all(attention.reshape(1, seq_devices, slice_rows, columns), SE...  25.5 us
    all_to_all x3, starting transfers between devices, to_positions(): lax.all_to_all(rows, SEQ_AXES, split_axis=0, concat_axis=0, tiled=True)  22.9 us
    all_to_all x3, starting transfers between devices, to_heads(): lax.all_to_all(head_rows(rows), SEQ_AXES, split_axis=0, concat_axis=0, ti...  20.8 us
    ppermute x2, waiting for transfers between devices, my_half(): received = lax.ppermute(theirs.astype(jnp.bfloat16), 'sx', partner)  20.5 us
    all_to_all x3, waiting for transfers between devices, to_positions(): lax.all_to_all(rows, SEQ_AXES, split_axis=0, concat_axis=0, tiled=True)  14.5 us
    all_to_all x1, waiting for transfers between devices, shards(): lax.all_to_all(x_sum.astype(jnp.bfloat16).reshape(z_size, z_rows, model_w...  12.4 us
    all_to_all x1, waiting for transfers between devices, shards(): lax.all_to_all(lax.all_to_all(delta_blocks, DP_AXES, split_axis=0, concat...  10.1 us
  transfers between devices with their start and end apart: 17, of which 11 were waited for; matrix products, arithmetic and copies ran while one was open for 36% of the time, Pallas kernels for 0%

profile of v2, /device:TPU:8, one launch (start us, length us, event | category | flops | bytes accessed | tf_op | source)
XLA Modules:
  0.0 380.7 jit_solution(8579282798412324548)
XLA Ops:
  10.1 11.4 %all-to-all-start = ((bf16[32,64,128]{2,1,0:T(8,128)(2,1)}), bf16[32,64,128]{2,1,0:T(8,128)(2,1)S(1)}, u32[]{:S(2)}, u32[]{:S(2)}) async-start(bf16[32,64,128]{2,1,0:T(8,128)(2,1)} %bitcast.1), calls=%async_computation | async-start | bytes 1048576 | tf_op jit(solution)/shard_map/all_to_all | solution.py:64
  22.8 16.5 %all-to-all-done = bf16[32,64,128]{2,1,0:T(8,128)(2,1)S(1)} async-done(((bf16[32,64,128]{2,1,0:T(8,128)(2,1)}), bf16[32,64,128]{2,1,0:T(8,128)(2,1)S(1)}, u32[]{:S(2)}, u32[]{:S(2)}) %all-to-all-start) | async-done | bytes 524320 | tf_op jit(solution)/shard_map/all_to_all | solution.py:64
  39.3 4.8 %all-to-all-start.4 = ((bf16[32,64,128]{2,1,0:T(8,128)(2,1)}), bf16[32,64,128]{2,1,0:T(8,128)(2,1)S(1)}, u32[]{:S(2)}, u32[]{:S(2)}) async-start(bf16[32,64,128]{2,1,0:T(8,128)(2,1)} %bitcast.363), calls=%async_computation.4 | async-start | bytes 1048576 | tf_op jit(solution)/shard_map/all_to_all | solution.py:64
  47.8 13.2 %all-to-all-done.4 = bf16[32,64,128]{2,1,0:T(8,128)(2,1)S(1)} async-done(((bf16[32,64,128]{2,1,0:T(8,128)(2,1)}), bf16[32,64,128]{2,1,0:T(8,128)(2,1)S(1)}, u32[]{:S(2)}, u32[]{:S(2)}) %all-to-all-start.4) | async-done | bytes 524320 | tf_op jit(solution)/shard_map/all_to_all | solution.py:64
  61.8 4.5 %all-to-all-start.1 = ((bf16[32,64,128]{2,1,0:T(8,128)(2,1)}), bf16[32,64,128]{2,1,0:T(8,128)(2,1)S(1)}, u32[]{:S(2)}, u32[]{:S(2)}) async-start(bf16[32,64,128]{2,1,0:T(8,128)(2,1)} %bitcast.365), calls=%async_computation.1 | async-start | bytes 1048576 | tf_op jit(solution)/shard_map/all_to_all | solution.py:64
  69.8 13.5 %all-to-all-done.1 = bf16[32,64,128]{2,1,0:T(8,128)(2,1)S(1)} async-done(((bf16[32,64,128]{2,1,0:T(8,128)(2,1)}), bf16[32,64,128]{2,1,0:T(8,128)(2,1)S(1)}, u32[]{:S(2)}, u32[]{:S(2)}) %all-to-all-start.1) | async-done | bytes 524320 | tf_op jit(solution)/shard_map/all_to_all | solution.py:64
  89.0 7.6 %collective-permute-done = bf16[32,64,128]{2,1,0:T(8,128)(2,1)} collective-permute-done((bf16[32,64,128]{2,1,0:T(8,128)(2,1)S(1)}, bf16[32,64,128]{2,1,0:T(8,128)(2,1)}, u32[]{:S(2)}, u32[]{:S(2)}) %collective-permute-start) | collective-permute-done | bytes 524320 | tf_op jit(solution)/shard_map/ppermute | solution.py:58
  123.6 25.5 %all_to_all.71 = bf16[1,32,64,128]{3,2,0,1:T(8,128)(2,1)} all-to-all(bf16[1,32,64,128]{3,2,0,1:T(8,128)(2,1)S(1)} %bitcast.378), channel_id=1, replica_groups=mesh['sz'=8,'sx'=4,'dy'=4,'dc'=2] {'sz','sx'}, dimensions={1} | all-to-all | bytes 1048576 | tf_op jit(solution)/shard_map/all_to_all | solution.py:137
  149.2 4.9 %all-to-all-start.9 = ((bf16[1,32,64,128]{3,2,0,1:T(8,128)(2,1)}), bf16[1,32,64,128]{3,2,0,1:T(8,128)(2,1)}, u32[]{:S(2)}, u32[]{:S(2)}) async-start(bf16[1,32,64,128]{3,2,0,1:T(8,128)(2,1)} %all_to_all.71), calls=%async_computation.9 | async-start | bytes 1048576 | tf_op jit(solution)/shard_map/all_to_all | solution.py:136
  154.1 4.9 %fusion.40 = bf16[8,2,2,64,128]{4,3,2,0,1:T(8,128)(2,1)S(1)} fusion(bf16[2,128,4096,1,1]{2,1,4,3,0:T(8,128)(2,1)S(1)} %bitcast.337, bf16[8,2,64,4096,1]{3,2,1,0,4:T(8,128)(2,1)} %bitcast.357), kind=kOutput, calls=%fused_computation.67 | convolution fusion | flops 2147745792 | bytes 11010048 | tf_op jit(solution)/shard_map/kptd,gcd->kgptc/dot_general | solution.py:154
  163.1 5.5 %all-to-all-start.2 = ((bf16[8,4,64,128]{3,2,1,0:T(8,128)(2,1)}), bf16[8,4,64,128]{3,2,1,0:T(8,128)(2,1)}, u32[]{:S(2)}, u32[]{:S(2)}) async-start(bf16[8,4,64,128]{3,2,1,0:T(8,128)(2,1)} %bitcast.29), calls=%async_computation.2 | async-start | bytes 1048576 | tf_op jit(solution)/shard_map/all_to_all | solution.py:183
  171.3 6.3 %all-to-all-done.2 = bf16[8,4,64,128]{3,2,1,0:T(8,128)(2,1)} async-done(((bf16[8,4,64,128]{3,2,1,0:T(8,128)(2,1)}), bf16[8,4,64,128]{3,2,1,0:T(8,128)(2,1)}, u32[]{:S(2)}, u32[]{:S(2)}) %all-to-all-start.2) | async-done | bytes 524320 | tf_op jit(solution)/shard_map/all_to_all | solution.py:183
  177.5 4.8 %all-to-all-start.3 = ((bf16[1,32,64,128]{3,2,0,1:T(8,128)(2,1)}), bf16[1,32,64,128]{3,2,0,1:T(8,128)(2,1)}, u32[]{:S(2)}, u32[]{:S(2)}) async-start(bf16[1,32,64,128]{3,2,0,1:T(8,128)(2,1)} %bitcast.31), calls=%async_computation.3 | async-start | bytes 1048576 | tf_op jit(solution)/shard_map/all_to_all | solution.py:182
  182.4 5.9 %fusion.4 = bf16[256,4096]{1,0:T(8,128)(2,1)S(1)} fusion(bf16[256,8,2,64]{0,3,2,1:T(8,128)(2,1)} %dot_general.135, bf16[8,2,64,4096]{3,2,1,0:T(8,128)(2,1)} %bitcast.358), kind=kOutput, calls=%fused_computation.12 | convolution fusion | flops 2148532224 | bytes 11010048 | tf_op jit(solution)/shard_map/kgptc,kptd->gcd/dot_general | solution.py:159
  189.8 10.1 %all-to-all-done.3 = bf16[1,32,64,128]{3,2,0,1:T(8,128)(2,1)} async-done(((bf16[1,32,64,128]{3,2,0,1:T(8,128)(2,1)}), bf16[1,32,64,128]{3,2,0,1:T(8,128)(2,1)}, u32[]{:S(2)}, u32[]{:S(2)}) %all-to-all-start.3) | async-done | bytes 524320 | tf_op jit(solution)/shard_map/all_to_all | solution.py:182
  200.0 4.6 %all-to-all-start.10 = ((bf16[4,8,8,4096]{3,2,1,0:T(8,128)(2,1)}), bf16[4,8,8,4096]{3,2,1,0:T(8,128)(2,1)}, u32[]{:S(2)}, u32[]{:S(2)}) async-start(bf16[4,8,8,4096]{3,2,1,0:T(8,128)(2,1)} %bitcast.334), calls=%async_computation.10 | async-start | bytes 4194304 | tf_op jit(solution)/shard_map/all_to_all | solution.py:166
  206.7 5.0 %fusion.25 = f32[64,64,128]{2,0,1:T(8,128)S(1)} fusion(f32[32,6,64,128]{3,2,1,0:T(8,128)S(1)} %bitcast.346, s32[32,6]{0,1:T(8,128)S(1)} %pad_add_fusion), kind=kOutput, calls=%fused_computation.49 | convolution fusion | flops 603992064 | bytes 8389376 | tf_op jit(solution)/shard_map/bjc,bjke->cke/dot_general | solution.py:253
  255.0 12.4 %all-to-all-done.11 = bf16[8,8,4096]{2,1,0:T(8,128)(2,1)} async-done(((bf16[8,8,4096]{2,1,0:T(8,128)(2,1)}), bf16[8,8,4096]{2,1,0:T(8,128)(2,1)}, u32[]{:S(2)}, u32[]{:S(2)}) %all-to-all-start.11) | async-done | bytes 524320 | tf_op jit(solution)/shard_map/all_to_all | solution.py:176
  277.9 4.6 %all-to-all-start.5 = ((bf16[32,64,128]{2,1,0:T(8,128)(2,1)}), bf16[32,64,128]{2,1,0:T(8,128)(2,1)S(1)}, u32[]{:S(2)}, u32[]{:S(2)}) async-start(bf16[32,64,128]{2,1,0:T(8,128)(2,1)} %bitcast.61), calls=%async_computation.5 | async-start | bytes 1048576 | tf_op jit(solution)/shard_map/all_to_all | solution.py:308
  285.4 5.0 %fusion.22 = f32[64,64,128]{2,0,1:T(8,128)S(1)} fusion(f32[32,6,64,128]{3,2,1,0:T(8,128)S(1)} %broadcast_multiply_fusion, s32[32,6]{0,1:T(8,128)S(1)} %pad_add_fusion), kind=kOutput, calls=%fused_computation.48 | convolution fusion | flops 603992064 | bytes 8389376 | tf_op jit(solution)/shard_map/bjc,bjke->cke/dot_general | solution.py:253
  309.7 9.9 %all-to-all-start.7 = ((bf16[32,64,128]{2,1,0:T(8,128)(2,1)}), bf16[32,64,128]{2,1,0:T(8,128)(2,1)S(1)}, u32[]{:S(2)}, u32[]{:S(2)}) async-start(bf16[32,64,128]{2,1,0:T(8,128)(2,1)} %fusion.51), calls=%async_computation.7 | async-start | bytes 1048576 | tf_op jit(solution)/shard_map/all_to_all | solution.py:308
  321.6 20.5 %collective-permute-done.2 = bf16[32,64,128]{2,1,0:T(8,128)(2,1)S(1)} collective-permute-done((bf16[32,64,128]{2,1,0:T(8,128)(2,1)S(1)}, bf16[32,64,128]{2,1,0:T(8,128)(2,1)S(1)}, u32[]{:S(2)}, u32[]{:S(2)}) %collective-permute-start.2) | collective-permute-done | bytes 524320 | tf_op jit(solution)/shard_map/ppermute | solution.py:304
  343.1 8.5 %all-to-all-start.6 = ((bf16[32,64,128]{2,1,0:T(8,128)(2,1)}), bf16[32,64,128]{2,1,0:T(8,128)(2,1)S(1)}, u32[]{:S(2)}, u32[]{:S(2)}) async-start(bf16[32,64,128]{2,1,0:T(8,128)(2,1)} %fusion.52), calls=%async_computation.6 | async-start | bytes 1048576 | tf_op jit(solution)/shard_map/all_to_all | solution.py:308
  354.3 14.5 %all-to-all-done.6 = bf16[32,64,128]{2,1,0:T(8,128)(2,1)S(1)} async-done(((bf16[32,64,128]{2,1,0:T(8,128)(2,1)}), bf16[32,64,128]{2,1,0:T(8,128)(2,1)S(1)}, u32[]{:S(2)}, u32[]{:S(2)}) %all-to-all-start.6) | async-done | bytes 524320 | tf_op jit(solution)/shard_map/all_to_all | solution.py:308
  (173 shorter events, 141.1 us)
Async XLA Ops:
  7.2 146.9 %copy-start = (bf16[256,4096]{1,0:T(8,128)(2,1)S(1)}, bf16[256,4096]{1,0:T(8,128)(2,1)}, u32[]{:S(2)}) copy-start(bf16[256,4096]{1,0:T(8,128)(2,1)} %param.15) | copy-start | bytes 6291460
  7.2 14.3 %copy-start.23 = (bf16[1,128,2048]{2,1,0:T(8,128)(2,1)S(1)}, bf16[1,128,2048]{2,1,0:T(8,128)(2,1)}, u32[]{:S(2)}) copy-start(bf16[1,128,2048]{2,1,0:T(8,128)(2,1)} %param.11) | copy-start | bytes 1572868
  7.2 146.9 %all-gather.3.cloned.1.call-start = ((), (), s32[]{:S(2)}) async-start(), calls=%async_computation.12 | async-start | bytes 9437184 | tf_op jit(solution)/shard_map/all_gather | solution.py:151
  10.0 34.2 %copy-start.25 = (s32[1,64,3]{1,0,2:T(1,128)S(1)}, s32[1,64,3]{1,0,2:T(1,128)}, u32[]{:S(2)}) copy-start(s32[1,64,3]{1,0,2:T(1,128)} %param.13) | copy-start | bytes 2308
  10.1 29.2 %all-to-all-start = ((bf16[32,64,128]{2,1,0:T(8,128)(2,1)}), bf16[32,64,128]{2,1,0:T(8,128)(2,1)S(1)}, u32[]{:S(2)}, u32[]{:S(2)}) async-start(bf16[32,64,128]{2,1,0:T(8,128)(2,1)} %bitcast.1), calls=%async_computation | async-start | bytes 1048576 | tf_op jit(solution)/shard_map/all_to_all | solution.py:64
  39.3 27.1 %copy-start.24 = (s32[1,128]{1,0:T(1,128)S(1)}, s32[1,128]{1,0:T(1,128)}, u32[]{:S(2)}) copy-start(s32[1,128]{1,0:T(1,128)} %param.14) | copy-start | bytes 1540
  39.3 21.8 %all-to-all-start.4 = ((bf16[32,64,128]{2,1,0:T(8,128)(2,1)}), bf16[32,64,128]{2,1,0:T(8,128)(2,1)S(1)}, u32[]{:S(2)}, u32[]{:S(2)}) async-start(bf16[32,64,128]{2,1,0:T(8,128)(2,1)} %bitcast.363), calls=%async_computation.4 | async-start | bytes 1048576 | tf_op jit(solution)/shard_map/all_to_all | solution.py:64
  61.8 21.5 %all-to-all-start.1 = ((bf16[32,64,128]{2,1,0:T(8,128)(2,1)}), bf16[32,64,128]{2,1,0:T(8,128)(2,1)S(1)}, u32[]{:S(2)}, u32[]{:S(2)}) async-start(bf16[32,64,128]{2,1,0:T(8,128)(2,1)} %bitcast.365), calls=%async_computation.1 | async-start | bytes 1048576 | tf_op jit(solution)/shard_map/all_to_all | solution.py:64
  67.2 19.3 %collective-permute-start.1 = (bf16[32,64,128]{2,1,0:T(8,128)(2,1)}, bf16[32,64,128]{2,1,0:T(8,128)(2,1)}, u32[]{:S(2)}, u32[]{:S(2)}) collective-permute-start(bf16[32,64,128]{2,1,0:T(8,128)(2,1)} %copy-done.22), channel_id=1, source_target_pairs={{0,8},{8,0},{16,24},{24,16},{1,9},{9,1},{17,25},{25,17},{2,10},{10... | collective-permute-start | bytes 1572872 | tf_op jit(solution)/shard_map/ppermute | solution.py:58
  69.1 27.5 %collective-permute-start = (bf16[32,64,128]{2,1,0:T(8,128)(2,1)S(1)}, bf16[32,64,128]{2,1,0:T(8,128)(2,1)}, u32[]{:S(2)}, u32[]{:S(2)}) collective-permute-start(bf16[32,64,128]{2,1,0:T(8,128)(2,1)S(1)} %all-to-all-done), channel_id=1, source_target_pairs={{0,8},{8,0},{16,24},{24,16},{1,9},{9,1},{17,25},{25,17},{2,10},{10... | collective-permute-start | bytes 1572872 | tf_op jit(solution)/shard_map/ppermute | solution.py:58
  149.2 13.9 %all-to-all-start.9 = ((bf16[1,32,64,128]{3,2,0,1:T(8,128)(2,1)}), bf16[1,32,64,128]{3,2,0,1:T(8,128)(2,1)}, u32[]{:S(2)}, u32[]{:S(2)}) async-start(bf16[1,32,64,128]{3,2,0,1:T(8,128)(2,1)} %all_to_all.71), calls=%async_computation.9 | async-start | bytes 1048576 | tf_op jit(solution)/shard_map/all_to_all | solution.py:136
  163.1 14.5 %all-to-all-start.2 = ((bf16[8,4,64,128]{3,2,1,0:T(8,128)(2,1)}), bf16[8,4,64,128]{3,2,1,0:T(8,128)(2,1)}, u32[]{:S(2)}, u32[]{:S(2)}) async-start(bf16[8,4,64,128]{3,2,1,0:T(8,128)(2,1)} %bitcast.29), calls=%async_computation.2 | async-start | bytes 1048576 | tf_op jit(solution)/shard_map/all_to_all | solution.py:183
  177.5 22.4 %all-to-all-start.3 = ((bf16[1,32,64,128]{3,2,0,1:T(8,128)(2,1)}), bf16[1,32,64,128]{3,2,0,1:T(8,128)(2,1)}, u32[]{:S(2)}, u32[]{:S(2)}) async-start(bf16[1,32,64,128]{3,2,0,1:T(8,128)(2,1)} %bitcast.31), calls=%async_computation.3 | async-start | bytes 1048576 | tf_op jit(solution)/shard_map/all_to_all | solution.py:182
  200.0 44.7 %all-to-all-start.10 = ((bf16[4,8,8,4096]{3,2,1,0:T(8,128)(2,1)}), bf16[4,8,8,4096]{3,2,1,0:T(8,128)(2,1)}, u32[]{:S(2)}, u32[]{:S(2)}) async-start(bf16[4,8,8,4096]{3,2,1,0:T(8,128)(2,1)} %bitcast.334), calls=%async_computation.10 | async-start | bytes 4194304 | tf_op jit(solution)/shard_map/all_to_all | solution.py:166
  229.4 77.4 %collective-permute-start.3 = (bf16[32,64,128]{2,1,0:T(8,128)(2,1)}, bf16[32,64,128]{2,1,0:T(8,128)(2,1)}, u32[]{:S(2)}, u32[]{:S(2)}) collective-permute-start(bf16[32,64,128]{2,1,0:T(8,128)(2,1)} %fusion.54), channel_id=1, source_target_pairs={{0,8},{8,0},{16,24},{24,16},{1,9},{9,1},{17,25},{25,17},{2,10},{10... | collective-permute-start | bytes 1572872 | tf_op jit(solution)/shard_map/ppermute | solution.py:304
  244.7 7.2 %copy-start.13 = (f32[128,4096]{1,0:T(8,128)S(1)}, f32[128,4096]{1,0:T(8,128)}, u32[]{:S(2)}) copy-start(f32[128,4096]{1,0:T(8,128)} %copy-done.10) | copy-start | bytes 6291460
  247.7 19.7 %all-to-all-start.11 = ((bf16[8,8,4096]{2,1,0:T(8,128)(2,1)}), bf16[8,8,4096]{2,1,0:T(8,128)(2,1)}, u32[]{:S(2)}, u32[]{:S(2)}) async-start(bf16[8,8,4096]{2,1,0:T(8,128)(2,1)} %reduce_sum.64), calls=%async_computation.11 | async-start | bytes 1048576 | tf_op jit(solution)/shard_map/all_to_all | solution.py:176
  251.8 118.5 %all-gather.5.cloned.1.call-start = ((), (), s32[]{:S(2)}) async-start(), calls=%async_computation.13 | async-start | bytes 2162688 | tf_op jit(solution)/shard_map/all_gather | solution.py:181
  275.2 7.3 %copy-start.20 = (bf16[32,64,128]{2,1,0:T(8,128)(2,1)S(1)}, bf16[32,64,128]{2,1,0:T(8,128)(2,1)}, u32[]{:S(2)}) copy-start(bf16[32,64,128]{2,1,0:T(8,128)(2,1)} %copy-done.19) | copy-start | bytes 1572868
  277.9 31.8 %all-to-all-start.5 = ((bf16[32,64,128]{2,1,0:T(8,128)(2,1)}), bf16[32,64,128]{2,1,0:T(8,128)(2,1)S(1)}, u32[]{:S(2)}, u32[]{:S(2)}) async-start(bf16[32,64,128]{2,1,0:T(8,128)(2,1)} %bitcast.61), calls=%async_computation.5 | async-start | bytes 1048576 | tf_op jit(solution)/shard_map/all_to_all | solution.py:308
  306.8 12.8 %copy-start.17 = (f32[4096,128]{1,0:T(8,128)S(1)}, f32[4096,128]{1,0:T(8,128)}, u32[]{:S(2)}) copy-start(f32[4096,128]{1,0:T(8,128)} %scatter_fusion) | copy-start | bytes 6291460
  309.7 33.4 %all-to-all-start.7 = ((bf16[32,64,128]{2,1,0:T(8,128)(2,1)}), bf16[32,64,128]{2,1,0:T(8,128)(2,1)S(1)}, u32[]{:S(2)}, u32[]{:S(2)}) async-start(bf16[32,64,128]{2,1,0:T(8,128)(2,1)} %fusion.51), calls=%async_computation.7 | async-start | bytes 1048576 | tf_op jit(solution)/shard_map/all_to_all | solution.py:308
  319.7 22.4 %collective-permute-start.2 = (bf16[32,64,128]{2,1,0:T(8,128)(2,1)S(1)}, bf16[32,64,128]{2,1,0:T(8,128)(2,1)S(1)}, u32[]{:S(2)}, u32[]{:S(2)}) collective-permute-start(bf16[32,64,128]{2,1,0:T(8,128)(2,1)S(1)} %fusion.53), channel_id=1, source_target_pairs={{0,8},{8,0},{16,24},{24,16},{1,9},{9,1},{17,25},{25,17},{2,10},{10... | collective-permute-start | bytes 1572872 | tf_op jit(solution)/shard_map/ppermute | solution.py:304
  343.1 25.7 %all-to-all-start.6 = ((bf16[32,64,128]{2,1,0:T(8,128)(2,1)}), bf16[32,64,128]{2,1,0:T(8,128)(2,1)S(1)}, u32[]{:S(2)}, u32[]{:S(2)}) async-start(bf16[32,64,128]{2,1,0:T(8,128)(2,1)} %fusion.52), calls=%async_computation.6 | async-start | bytes 1048576 | tf_op jit(solution)/shard_map/all_to_all | solution.py:308
  (20 other events, 65.9 us)
Sparse Core Ops, SparseCore 0:
  9.9 54.3 all-gather.2
  269.3 76.3 all-gather.4
